TPU v7x, 32 devices: a whole 2x2x4 slice. The times are simulated.
32 devices in a mesh: patch: 8 (over z, y), band: 4 (over x, core).
Axes of the slice: x: 2, y: 2, z: 4, core: 2. Of those that a mesh axis runs over, the one named last changes fastest.
Arguments:
- exposures: float32 [64, 256, 128], P(('band', 'patch')), parts along dimension 0, may hold values from -6 to 6
- variance: float32 [64, 256, 128], P(('band', 'patch')), parts along dimension 0, may hold values from 0.01 to 60, as said below
- mask_bits: int32 [64, 256, 128], P(('band', 'patch')), parts along dimension 0, may hold values from 0 to 4095
- kernel_coeffs: float32 [64, 27, 6], P(('band', 'patch')), parts along dimension 0, may hold values from -3 to 3
- ccd_visit: int32 [64, 1], P(('band', 'patch')), parts along dimension 0, may hold values from 0 to 7
- strip_patch: int32 [2048, 1], P(('band', 'patch')), parts along dimension 0, may hold values from 0 to 7, as said below
- strip_row: int32 [2048], P(('band', 'patch')), parts along dimension 0, may hold values from 0 to 120
- strip_col: int32 [2048], P(('band', 'patch')), parts along dimension 0, may hold values from 0 to 384
Outputs:
- coadd_image: float32 [32, 128, 512], P(('band', 'patch')), parts along dimension 0
- weight_map: float32 [32, 128, 512], P(('band', 'patch')), parts along dimension 0
There are 4 independent parts, one for each index of `band`. A program takes and returns all parts, laid end to end along the dimension named above; each array names one. Nothing has to cross between parts.
Inputs may be any that keep to these rules, and one draw needn't show every extreme that they name: `variance`: Positive. `ccd_visit`: every visit has at least one CCD. `strip_patch`: among the strips of one device (aligned blocks of 64 rows) no patch is named more than 16 times; one patch is named exactly 16 times in every block.
All inputs are finite; a program needn't handle non-finite values.
Results may differ from a plain program's by a relative error of at most 0.00011.
Values sent between devices are 32-bit elements; how exact they have to be, the bound alone decides.
No kernel may reach another device: no remote copies, remote signals or barrier semaphores. Data moves between devices by JAX's collectives and lax.ppermute only.
A program may use at most 64 MiB of HBM per device.

v0:
```python
import math
import jax
import numpy as np
import jax.numpy as jnp
from jax import lax
from jax.sharding import PartitionSpec as P

PH = 128
PW = 512
KS = 21
VISITS = 8
gauss_widths = (0.75, 1.5, 3.0)
largest_value = lax.Precision.HIGHEST
mxu_value = lax.Precision.HIGH


def tap_table(kernel_half_width):
    support = np.arange(-kernel_half_width, kernel_half_width + 1).astype(np.float64)
    tables = []
    for spread in gauss_widths:
        s32 = float(np.float32(spread))
        gauss_total = np.sum(np.exp(-support * support / (2.0 * s32 * s32)))
        profile = np.exp(-support * support / (2.0 * s32 * s32)) / gauss_total
        scaled = support / s32
        tables.append(np.stack([profile, profile * scaled, profile * scaled * scaled]))
    return np.stack(tables)


def row_blocks(block_rows, window_rows, kernel_half_width):
    taps = tap_table(kernel_half_width).reshape(9, 2 * kernel_half_width + 1)
    out = np.zeros((9, block_rows, window_rows), np.float64)
    for i in range(block_rows):
        out[:, i, i : i + 2 * kernel_half_width + 1] = taps
    return out.astype(np.float32)


def column_ops(column_count, kernel_half_width):
    taps = tap_table(kernel_half_width)
    out = np.zeros((3, 3, column_count, column_count), np.float64)
    for y in range(column_count):
        lo = max(0, y - kernel_half_width)
        hi = min(column_count, y + kernel_half_width + 1)
        for x in range(lo, hi):
            out[:, :, y, x] = taps[:, :, y - x + kernel_half_width]
    return out.astype(np.float32)


def convolve_all(exposures, kernel_coeffs):
    kernel_half_width = KS // 2
    n, height, columns = exposures.shape
    block = 8
    blocks = height // block
    span = 2 * kernel_half_width + block
    reach = -(-span // block)
    total_rows = (blocks + reach - 1) * block
    padded = jnp.pad(
        exposures, ((0, 0), (kernel_half_width, total_rows - height - kernel_half_width), (0, 0))
    ).reshape(n, blocks + reach - 1, block, columns)
    windows = jnp.concatenate([padded[:, j : j + blocks] for j in range(reach)], axis=2)
    rows = jnp.asarray(row_blocks(block, reach * block, kernel_half_width))
    smooth = jnp.einsum("kit,nqtx->nqkix", rows, windows, precision=mxu_value)
    col_ops = jnp.asarray(column_ops(columns, kernel_half_width))
    x_line = 2.0 * jnp.arange(columns).astype(jnp.float32) / (columns - 1) - 1.0
    coef = kernel_coeffs.reshape(n, 3, 3, 3, 6)
    c = [coef[..., p, None] for p in range(6)]
    fx = jnp.stack(
        [
            c[0] + c[1] * x_line + c[3] * (x_line * x_line),
            c[2] + c[4] * x_line,
            jnp.broadcast_to(c[5], c[0].shape[:-1] + (columns,)),
        ],
        axis=4,
    )
    mixed = jnp.sum(col_ops[None, :, None, :, :, None, :] * fx[:, :, :, :, None, :, :], axis=3)
    mixed = mixed.reshape(n, 9, columns, 3 * columns)
    fields = jnp.einsum("nqkiy,nkyz->nqiz", smooth, mixed, precision=mxu_value)
    fields = fields.reshape(n, height, 3 * columns)
    y_line = (2.0 * jnp.arange(height).astype(jnp.float32) / (height - 1) - 1.0)[None, :, None]
    return (
        fields[:, :, :columns]
        + y_line * fields[:, :, columns : 2 * columns]
        + y_line * y_line * fields[:, :, 2 * columns :]
    )


def place_slots(flux_flat, weight_flat, offsets, patch_rows, patch_cols):
    slot_total, strip_rows, columns = flux_flat.shape
    group = math.gcd(slot_total, 16)
    pairs = jnp.stack([flux_flat, weight_flat], axis=1).reshape(
        slot_total // group, group, 2, strip_rows, columns
    )
    grouped_offsets = offsets.reshape(slot_total // group, group, offsets.shape[1])
    target_cols = jnp.arange(patch_cols)
    source_cols = jnp.arange(columns)
    target_rows = jnp.arange(patch_rows)
    source_rows = jnp.arange(strip_rows)

    def place_group(total, item):
        pixel_block_tile, block_offsets = item
        column_selection = (
            target_cols[None, None, :]
            == block_offsets[:, 1][:, None, None] + source_cols[None, :, None]
        ).astype(jnp.float32)
        row_select = (
            target_rows[None, :, None]
            == block_offsets[:, 0][:, None, None] + source_rows[None, None, :]
        ).astype(jnp.float32)
        broadened_width = jnp.einsum(
            "vmwn,vny->vmwy", pixel_block_tile, column_selection, precision=largest_value
        )
        return (
            total
            + jnp.einsum("gri,gkip->krp", row_select, broadened_width, precision=largest_value),
            None,
        )

    start = jnp.zeros((2, patch_rows, patch_cols), jnp.float32)
    placed, _ = lax.scan(place_group, start, (pairs, grouped_offsets))
    return (placed[0], placed[1])


def shards(
    exposures, variance, mask_bits, kernel_coeffs, ccd_visit, strip_patch, strip_row, strip_col
):
    ccd_count, height, columns = exposures.shape
    strip_total = strip_patch.shape[0]
    per_ccd = strip_total // ccd_count
    strip_rows = height // per_ccd
    devices = lax.axis_size("patch")
    capacity = 2 * strip_total // devices
    usable = (jnp.bitwise_and(mask_bits, 3) != 3).astype(jnp.float32)
    visit_hot = (ccd_visit == jnp.arange(VISITS)[None, :]).astype(jnp.float32)
    local_count = jnp.sum(jnp.sum(usable, axis=(1, 2))[:, None] * visit_hot, axis=0)
    local_load = jnp.sum(jnp.sum(usable * variance, axis=(1, 2))[:, None] * visit_hot, axis=0)
    destination = strip_patch[:, 0]
    strip_ids = jnp.arange(strip_total)
    earlier = strip_ids[None, :] < strip_ids[:, None]
    same_target = destination[None, :] == destination[:, None]
    slot_rank = jnp.sum(jnp.logical_and(earlier, same_target).astype(jnp.int32), axis=1)
    slot_index = destination * capacity + slot_rank
    slot_total = devices * capacity
    chooser = (slot_index[None, :] == jnp.arange(slot_total)[:, None]).astype(jnp.float32)
    strip_visit = jnp.repeat(ccd_visit[:, 0], per_ccd)
    placement = jnp.stack([strip_row, strip_col, strip_visit], axis=1).astype(jnp.float32)
    slot_meta = jnp.dot(chooser, placement, precision=largest_value).reshape(devices, capacity, 3)
    meta = jnp.zeros((devices, 8, columns), jnp.float32)
    meta = meta.at[:, 0:3, :capacity].set(jnp.swapaxes(slot_meta, 1, 2))
    meta = meta.at[:, 3, :VISITS].set(jnp.broadcast_to(local_count, (devices, VISITS)))
    meta = meta.at[:, 4, :VISITS].set(jnp.broadcast_to(local_load, (devices, VISITS)))
    body_rows = capacity * strip_rows
    weight_tiles = usable.reshape(strip_total, strip_rows * columns)
    weight_packed = jnp.dot(chooser, weight_tiles, precision=largest_value).reshape(
        devices, body_rows, columns
    )
    first = jnp.concatenate([weight_packed, meta], axis=1)
    got_first = lax.all_to_all(first, "patch", split_axis=0, concat_axis=0, tiled=True)
    convolved = convolve_all(exposures, kernel_coeffs)
    flux_tiles = (usable * convolved).reshape(strip_total, strip_rows * columns)
    flux_packed = jnp.dot(chooser, flux_tiles, precision=largest_value).reshape(
        devices, body_rows, columns
    )
    got_flux = lax.all_to_all(flux_packed, "patch", split_axis=0, concat_axis=0, tiled=True)
    got_meta = got_first[:, body_rows:, :]
    visit_count = jnp.sum(got_meta[:, 3, :VISITS], axis=0)
    visit_load = jnp.sum(got_meta[:, 4, :VISITS], axis=0)
    visit_weight = (visit_count + 1.0) / (visit_load + 1.0)
    slot_rows = got_meta[:, 0, :capacity].reshape(slot_total).astype(jnp.int32)
    slot_cols = got_meta[:, 1, :capacity].reshape(slot_total).astype(jnp.int32)
    slot_visit = got_meta[:, 2, :capacity].reshape(slot_total).astype(jnp.int32)
    slot_hot = (slot_visit[:, None] == jnp.arange(VISITS)[None, :]).astype(jnp.float32)
    slot_weight = jnp.sum(slot_hot * visit_weight[None, :], axis=1)
    weight_body = got_first[:, :body_rows, :].reshape(slot_total, strip_rows, columns)
    flux_body = got_flux.reshape(slot_total, strip_rows, columns)
    weight_body = weight_body * slot_weight[:, None, None]
    flux_body = flux_body * slot_weight[:, None, None]
    offsets = jnp.stack([slot_rows, slot_cols], axis=1)
    numerator, weight_map = place_slots(flux_body, weight_body, offsets, PH, PW)
    coadd_image = numerator / jnp.maximum(weight_map, 1.0)
    return (coadd_image[None], weight_map[None])


def solution(mesh):
    return jax.shard_map(
        shards,
        mesh=mesh,
        in_specs=(
            P(("band", "patch"), None, None),
            P(("band", "patch"), None, None),
            P(("band", "patch"), None, None),
            P(("band", "patch"), None, None),
            P(("band", "patch"), None),
            P(("band", "patch"), None),
            P(("band", "patch")),
            P(("band", "patch")),
        ),
        out_specs=(P(("band", "patch"), None, None), P(("band", "patch"), None, None)),
        check_vma=False,
    )
```

profile of v0, /device:TPU:0, one launch (start us, length us, event | category | flops | bytes accessed | tf_op | source)
XLA Modules:
  0.0 81.9 jit_solution(7379162448762953336)
XLA Ops:
  0.7 0.8 copy.70
  1.4 0.2 fusion.51
  1.7 0.2 copy.71
  1.9 0.2 copy.73
  2.1 0.2 copy.75
  2.3 0.2 copy.77
  2.6 0.2 copy.79
  2.8 0.2 copy.81
  3.0 0.4 multiply_add_fusion.1
  3.6 4.2 %multiply_reduce_fusion = f32[2,3,3,128,3,128]{5,3,4,2,1,0:T(8,128)} fusion(f32[2,3,3,3,3,128]{5,4,3,2,1,0:T(4,128)S(1)} %pad_maximum_fusion.2, f32[3,3,128,128]{3,2,1,0:T(8,128)} %constant.143.clone), kind=kLoop, calls=%fused_computation.20 | loop fusion | flops 4423680 | bytes 4211712 | tf_op jit(solution)/shard_map/reduce_sum | solution.py:74
  7.8 3.3 %copy.83 = f32[2,3,3,128,3,128]{3,5,4,2,1,0:T(8,128)S(1)} copy(f32[2,3,3,128,3,128]{5,3,4,2,1,0:T(8,128)} %multiply_reduce_fusion) | data formatting | bytes 7077888 | tf_op jit(solution)/shard_map/reduce_sum | solution.py:74
  11.1 1.0 %pad_bitcast_fusion = f32[2,35,8,128]{3,2,1,0:T(8,128)S(1)} fusion(f32[2,256,128]{2,1,0:T(8,128)} %param.18), kind=kLoop, calls=%fused_computation.37 | loop fusion | bytes 548864 | tf_op jit(solution)/shard_map/reshape | solution.py:58
  12.1 1.8 %fusion.22 = f32[2,32,128,9,8]{2,4,3,1,0:T(8,128)S(1)} fusion(f32[9,8,32,1,1]{2,1,0,4,3:T(8,128)} %constant.153, f32[2,32,8,128]{3,2,1,0:T(8,128)S(1)} %get-tuple-element.177, f32[2,32,8,128]{3,2,1,0:T(8,128)S(1)} %get-tuple-element.178, f32[2,32,8,128]{3,2,1,0:T(8,128)S(1)} %get-tuple-element.179, f32[2,32,8,128]{3,2,1,0:T(8,128)S(1)} %get-tuple-element.176), kind=kOutput, calls=%fused_computation.25 | convolution fusion | flops 114032640 | bytes 3417088 | tf_op jit(solution)/shard_map/kit,nqtx->nqkix/dot_general | solution.py:61
  14.0 2.3 %fusion.19 = f32[2,256,384]{2,1,0:T(8,128)S(1)} fusion(f32[2,9,128,384,1]{2,3,1,4,0:T(8,128)S(1)} %bitcast.101, f32[2,32,128,9,8]{2,4,3,1,0:T(8,128)S(1)} %fusion.22), kind=kOutput, calls=%fused_computation.23 | convolution fusion | flops 1358954496 | bytes 6684672 | tf_op jit(solution)/shard_map/nqkiy,nkyz->nqiz/dot_general | solution.py:76
  16.3 0.1 fusion.31
  16.5 1.1 %select_reduce_fusion = (f32[2]{0:T(128)S(1)}, f32[2]{0:T(128)S(1)}) fusion(pred[2,256,128]{2,1,0:T(32,128)(4,1)S(1)} %get-tuple-element.171, f32[2,256,128]{2,1,0:T(8,128)} %param.19), kind=kLoop, calls=%fused_computation.44 | loop fusion | flops 262140 | bytes 327696 | tf_op jit(solution)/shard_map/reduce_sum | solution.py:134
  17.6 0.2 convert_reduce_fusion.1
  18.0 0.8 fusion.33
  18.9 0.2 fusion.34
  19.4 0.3 scatter.11
  19.7 0.3 scatter.14
  19.9 0.8 %pad_maximum_fusion.1 = f32[8,136,128]{2,1,0:T(8,128)} fusion(f32[8,8,128]{2,1,0:T(8,128)S(1)} %scatter.14, f32[8,128,128]{2,1,0:T(8,128)S(1)} %reshape.332), kind=kLoop, calls=%fused_computation.33 | loop fusion | flops 139264 | bytes 1114112 | tf_op jit(solution)/shard_map/concatenate | solution.py:155
  20.8 7.3 %all-to-all-start.1 = ((f32[8,136,128]{2,1,0:T(8,128)}), f32[8,136,128]{2,1,0:T(8,128)S(1)}, u32[]{:S(2)}, u32[]{:S(2)}) async-start(f32[8,136,128]{2,1,0:T(8,128)} %pad_maximum_fusion.1), calls=%async_computation.1 | async-start | bytes 1114112 | tf_op jit(solution)/shard_map/all_to_all | solution.py:156
  28.1 0.4 fusion.35
  28.5 0.9 %reshape.329 = f32[8,128,128]{2,1,0:T(8,128)} reshape(f32[128,1024]{1,0:T(8,128)S(1)} %fusion.35) | data formatting | bytes 1048576 | tf_op jit(solution)/shard_map/reshape | solution.py:159
  29.4 13.9 %all-to-all-done.1 = f32[8,136,128]{2,1,0:T(8,128)S(1)} async-done(((f32[8,136,128]{2,1,0:T(8,128)}), f32[8,136,128]{2,1,0:T(8,128)S(1)}, u32[]{:S(2)}, u32[]{:S(2)}) %all-to-all-start.1) | async-done | bytes 557088 | tf_op jit(solution)/shard_map/all_to_all | solution.py:156
  43.3 3.6 %all-to-all-start = ((f32[8,128,128]{2,1,0:T(8,128)}), f32[8,128,128]{2,1,0:T(8,128)S(1)}, u32[]{:S(2)}, u32[]{:S(2)}) async-start(f32[8,128,128]{2,1,0:T(8,128)} %reshape.329), calls=%async_computation | async-start | bytes 1048576 | tf_op jit(solution)/shard_map/all_to_all | solution.py:162
  47.3 14.3 %all-to-all-done = f32[8,128,128]{2,1,0:T(8,128)S(1)} async-done(((f32[8,128,128]{2,1,0:T(8,128)}), f32[8,128,128]{2,1,0:T(8,128)S(1)}, u32[]{:S(2)}, u32[]{:S(2)}) %all-to-all-start) | async-done | bytes 524320 | tf_op jit(solution)/shard_map/all_to_all | solution.py:162
  61.6 0.2 bitcast_multiply_fusion
  61.9 19.0 %while.16 = (s32[]{:T(128)}, f32[2,128,512]{1,2,0:T(8,128)S(1)}, f32[8,16,2,8,128]{4,3,2,1,0:T(8,128)S(1)}, s32[8,16,2]{1,0,2:T(8,128)S(1)}, s32[]{:T(128)}, /*index=5*/s32[]{:T(128)}) while((s32[]{:T(128)}, f32[2,128,512]{1,2,0:T(8,128)S(1)}, f32[8,16,2,8,128]{4,3,2,1,0:T(8,128)S(1)}, s32[8,16,2]{1,0,2:T(8,128)S(1)}, ...), condition=%wide.region_10.11_spmd.clone.clone, body=%wide.region_9.10_spmd.clone.clone.sunk | while | flops 403982464 | bytes 2246359 | solution.py:118
  62.0 1.5 %fusion.67 = f32[16,2,8,512]{3,2,1,0:T(8,128)S(1)} fusion(s32[16,128]{1,0:T(8,128)S(1)} %iota_add_fusion.4, f32[8,16,2,8,128]{4,3,2,1,0:T(8,128)S(1)} %get-tuple-element.237, s32[]{:T(128)} %get-tuple-element.229), kind=kOutput, calls=%fused_computation.5.clone.1 | convolution fusion | flops 202375168 | bytes 663556 | tf_op jit(solution)/shard_map/while/body/eval_jaxpr/vmwn,vny->vmwy/dot_general | solution.py:108
  63.5 0.7 fusion.68
  64.3 1.5 %fusion.67 = f32[16,2,8,512]{3,2,1,0:T(8,128)S(1)} fusion(s32[16,128]{1,0:T(8,128)S(1)} %iota_add_fusion.4, f32[8,16,2,8,128]{4,3,2,1,0:T(8,128)S(1)} %get-tuple-element.237, s32[]{:T(128)} %get-tuple-element.229), kind=kOutput, calls=%fused_computation.5.clone.1 | convolution fusion | flops 202375168 | bytes 663556 | tf_op jit(solution)/shard_map/while/body/eval_jaxpr/vmwn,vny->vmwy/dot_general | solution.py:108
  65.9 0.7 fusion.68
  66.7 1.5 %fusion.67 = f32[16,2,8,512]{3,2,1,0:T(8,128)S(1)} fusion(s32[16,128]{1,0:T(8,128)S(1)} %iota_add_fusion.4, f32[8,16,2,8,128]{4,3,2,1,0:T(8,128)S(1)} %get-tuple-element.237, s32[]{:T(128)} %get-tuple-element.229), kind=kOutput, calls=%fused_computation.5.clone.1 | convolution fusion | flops 202375168 | bytes 663556 | tf_op jit(solution)/shard_map/while/body/eval_jaxpr/vmwn,vny->vmwy/dot_general | solution.py:108
  68.3 0.7 fusion.68
  69.1 1.5 %fusion.67 = f32[16,2,8,512]{3,2,1,0:T(8,128)S(1)} fusion(s32[16,128]{1,0:T(8,128)S(1)} %iota_add_fusion.4, f32[8,16,2,8,128]{4,3,2,1,0:T(8,128)S(1)} %get-tuple-element.237, s32[]{:T(128)} %get-tuple-element.229), kind=kOutput, calls=%fused_computation.5.clone.1 | convolution fusion | flops 202375168 | bytes 663556 | tf_op jit(solution)/shard_map/while/body/eval_jaxpr/vmwn,vny->vmwy/dot_general | solution.py:108
  70.6 0.7 fusion.68
  71.5 1.5 %fusion.67 = f32[16,2,8,512]{3,2,1,0:T(8,128)S(1)} fusion(s32[16,128]{1,0:T(8,128)S(1)} %iota_add_fusion.4, f32[8,16,2,8,128]{4,3,2,1,0:T(8,128)S(1)} %get-tuple-element.237, s32[]{:T(128)} %get-tuple-element.229), kind=kOutput, calls=%fused_computation.5.clone.1 | convolution fusion | flops 202375168 | bytes 663556 | tf_op jit(solution)/shard_map/while/body/eval_jaxpr/vmwn,vny->vmwy/dot_general | solution.py:108
  73.0 0.7 fusion.68
  73.8 1.5 %fusion.67 = f32[16,2,8,512]{3,2,1,0:T(8,128)S(1)} fusion(s32[16,128]{1,0:T(8,128)S(1)} %iota_add_fusion.4, f32[8,16,2,8,128]{4,3,2,1,0:T(8,128)S(1)} %get-tuple-element.237, s32[]{:T(128)} %get-tuple-element.229), kind=kOutput, calls=%fused_computation.5.clone.1 | convolution fusion | flops 202375168 | bytes 663556 | tf_op jit(solution)/shard_map/while/body/eval_jaxpr/vmwn,vny->vmwy/dot_general | solution.py:108
  75.4 0.7 fusion.68
  76.2 1.5 %fusion.67 = f32[16,2,8,512]{3,2,1,0:T(8,128)S(1)} fusion(s32[16,128]{1,0:T(8,128)S(1)} %iota_add_fusion.4, f32[8,16,2,8,128]{4,3,2,1,0:T(8,128)S(1)} %get-tuple-element.237, s32[]{:T(128)} %get-tuple-element.229), kind=kOutput, calls=%fused_computation.5.clone.1 | convolution fusion | flops 202375168 | bytes 663556 | tf_op jit(solution)/shard_map/while/body/eval_jaxpr/vmwn,vny->vmwy/dot_general | solution.py:108
  77.7 0.7 fusion.68
  78.6 1.5 %fusion.67 = f32[16,2,8,512]{3,2,1,0:T(8,128)S(1)} fusion(s32[16,128]{1,0:T(8,128)S(1)} %iota_add_fusion.4, f32[8,16,2,8,128]{4,3,2,1,0:T(8,128)S(1)} %get-tuple-element.237, s32[]{:T(128)} %get-tuple-element.229), kind=kOutput, calls=%fused_computation.5.clone.1 | convolution fusion | flops 202375168 | bytes 663556 | tf_op jit(solution)/shard_map/while/body/eval_jaxpr/vmwn,vny->vmwy/dot_general | solution.py:108
  80.1 0.7 fusion.68
  80.9 0.2 copy.90
  81.1 0.8 slice_divide_fusion
  (73 shorter events, 2.5 us)
Async XLA Ops:
  14.0 2.3 %copy-start = (s32[2,256,128]{2,1,0:T(8,128)S(1)}, s32[2,256,128]{2,1,0:T(8,128)}, u32[]{:S(2)}) copy-start(s32[2,256,128]{2,1,0:T(8,128)} %param.20) | copy-start | bytes 786436
  14.0 3.7 %copy-start.2 = (s32[64,1]{0,1:T(1,128)S(1)}, s32[64,1]{0,1:T(1,128)}, u32[]{:S(2)}) copy-start(s32[64,1]{0,1:T(1,128)} %param.23) | copy-start | bytes 772
  14.0 3.8 %copy-start.1 = (s32[2,1]{0,1:T(1,128)S(1)}, s32[2,1]{0,1:T(1,128)}, u32[]{:S(2)}) copy-start(s32[2,1]{0,1:T(1,128)} %param.22) | copy-start | bytes 28
  20.8 22.5 %all-to-all-start.1 = ((f32[8,136,128]{2,1,0:T(8,128)}), f32[8,136,128]{2,1,0:T(8,128)S(1)}, u32[]{:S(2)}, u32[]{:S(2)}) async-start(f32[8,136,128]{2,1,0:T(8,128)} %pad_maximum_fusion.1), calls=%async_computation.1 | async-start | bytes 1114112 | tf_op jit(solution)/shard_map/all_to_all | solution.py:156
  43.3 18.3 %all-to-all-start = ((f32[8,128,128]{2,1,0:T(8,128)}), f32[8,128,128]{2,1,0:T(8,128)S(1)}, u32[]{:S(2)}, u32[]{:S(2)}) async-start(f32[8,128,128]{2,1,0:T(8,128)} %reshape.329), calls=%async_computation | async-start | bytes 1048576 | tf_op jit(solution)/shard_map/all_to_all | solution.py:162
where the time goes:
time: 82.4 us; the launch traced here: 81.9 us
  waiting for transfers between devices  28.2 us (34%)
  matrix products  22.9 us (28%)
  starting transfers between devices  10.9 us (13%)
  other arithmetic  9.37 us (11%)
  local copies, waits for them, and re-layouts  9.19 us (11%)
  between operations  0.95 us (1%)
    all_to_all x1, waiting for transfers between devices, shards(): lax.all_to_all(flux_packed, 'patch', split_axis=0, concat_axis=0, tiled=T...  14.3 us
    all_to_all x1, waiting for transfers between devices, shards(): lax.all_to_all(first, 'patch', split_axis=0, concat_axis=0, tiled=True)  13.9 us
    dot_general x8, matrix products, place_group(): jnp.einsum('vmwn,vny->vmwy', pixel_block_tile, column_selection, precisio...  11.7 us
    all_to_all x1, starting transfers between devices, shards(): lax.all_to_all(first, 'patch', split_axis=0, concat_axis=0, tiled=True)  7.31 us
    dot_general x8, matrix products, place_group(): jnp.einsum('gri,gkip->krp', row_select, broadened_width, precision=larges...  5.76 us
    reduce_sum x1, other arithmetic, convolve_all(): jnp.sum(col_ops[None, :, None, :, :, None, :] * fx[:, :, :, :, None, :, :...  4.17 us
    all_to_all x1, starting transfers between devices, shards(): lax.all_to_all(flux_packed, 'patch', split_axis=0, concat_axis=0, tiled=T...  3.64 us
    reduce_sum x1, local copies, waits for them, and re-layouts, convolve_all(): jnp.sum(col_ops[None, :, None, :, :, None, :] * fx[:, :, :, :, None, :, :...  3.31 us
  transfers between devices with their start and end apart: 2, of which 2 were waited for; matrix products, arithmetic and copies ran while one was open for 2% of the time, Pallas kernels for 0%

commit v1 on v0

--- a/solution.py
+++ b/solution.py
@@ -159,7 +159,19 @@
     flux_packed = jnp.dot(chooser, flux_tiles, precision=largest_value).reshape(
         devices, body_rows, columns
     )
-    got_flux = lax.all_to_all(flux_packed, "patch", split_axis=0, concat_axis=0, tiled=True)
+    ways, here = (lax.axis_size("patch"), lax.axis_index("patch"))
+    width = flux_packed.shape[0] // ways
+    shape = list(flux_packed.shape)
+    shape[0] = width
+    height_2 = shape[0]
+    shape[0] = height_2 * ways
+    full = jnp.zeros(shape, flux_packed.dtype)
+    for mask in range(ways):
+        part = lax.dynamic_slice_in_dim(flux_packed, (here ^ mask) * width, width, axis=0)
+        if mask:
+            part = lax.ppermute(part, "patch", [(d, d ^ mask) for d in range(ways)])
+        full = lax.dynamic_update_slice_in_dim(full, part, (here ^ mask) * height_2, axis=0)
+    got_flux = full
     got_meta = got_first[:, body_rows:, :]
     visit_count = jnp.sum(got_meta[:, 3, :VISITS], axis=0)
     visit_load = jnp.sum(got_meta[:, 4, :VISITS], axis=0)

time: 82.4 us -> 74.8 us (0.908)
  waiting for transfers between devices: 28.2 us -> 9.01 us
  starting transfers between devices: 10.9 us -> 23.1 us
    ppermute x0 -> x7, starting transfers between devices: none -> 15.8 us  [shards(): part = lax.ppermute(part, 'patch', [(d, d ^ mask) for d in range(ways)])]
    all_to_all x1 -> x0, waiting for transfers between devices: 14.3 us -> none  [shards(): lax.all_to_all(flux_packed, 'patch', split_axis=0, concat_axis=0, tiled=T...]
    all_to_all x1, waiting for transfers between devices: 13.9 us -> 0.01 us  [shards(): lax.all_to_all(first, 'patch', split_axis=0, concat_axis=0, tiled=True)]
    ppermute x0 -> x7, waiting for transfers between devices: none -> 9.01 us  [shards(): part = lax.ppermute(part, 'patch', [(d, d ^ mask) for d in range(ways)])]
    all_to_all x1 -> x0, starting transfers between devices: 3.64 us -> none  [shards(): lax.all_to_all(flux_packed, 'patch', split_axis=0, concat_axis=0, tiled=T...]
  transfers between devices with their start and end apart: 2 -> 8, of which waited for: 2 -> 2; matrix products, arithmetic and copies ran while one was open for 2% -> 1% of each run, Pallas kernels for 0% -> 0%
where the time goes in v1:
time: 74.8 us; the launch traced here: 74.3 us
  starting transfers between devices  23.1 us (31%)
  matrix products  22.9 us (31%)
  other arithmetic  9.38 us (13%)
  waiting for transfers between devices  9.01 us (12%)
  local copies, waits for them, and re-layouts  8.56 us (11%)
  between operations  1.09 us (1%)
    ppermute x7, starting transfers between devices, shards(): part = lax.ppermute(part, 'patch', [(d, d ^ mask) for d in range(ways)])  15.8 us
    dot_general x8, matrix products, place_group(): jnp.einsum('vmwn,vny->vmwy', pixel_block_tile, column_selection, precisio...  11.7 us
    ppermute x7, waiting for transfers between devices, shards(): part = lax.ppermute(part, 'patch', [(d, d ^ mask) for d in range(ways)])  9.01 us
    all_to_all x1, starting transfers between devices, shards(): lax.all_to_all(first, 'patch', split_axis=0, concat_axis=0, tiled=True)  7.31 us
    dot_general x8, matrix products, place_group(): jnp.einsum('gri,gkip->krp', row_select, broadened_width, precision=larges...  5.76 us
    reduce_sum x1, other arithmetic, convolve_all(): jnp.sum(col_ops[None, :, None, :, :, None, :] * fx[:, :, :, :, None, :, :...  4.17 us
    reduce_sum x1, local copies, waits for them, and re-layouts, convolve_all(): jnp.sum(col_ops[None, :, None, :, :, None, :] * fx[:, :, :, :, None, :, :...  3.31 us
    dot_general x1, matrix products, convolve_all(): fields = jnp.einsum('nqkiy,nkyz->nqiz', smooth, mixed, precision=mxu_value)  2.27 us
  transfers between devices with their start and end apart: 8, of which 2 were waited for; matrix products, arithmetic and copies ran while one was open for 1% of the time, Pallas kernels for 0%

profile of v1, /device:TPU:0, one launch (start us, length us, event | category | flops | bytes accessed | tf_op | source)
XLA Modules:
  0.0 74.3 jit_solution(2636298272817304843)
XLA Ops:
  0.7 0.8 %copy.70 = f32[2,27,6]{2,0,1:T(2,128)S(1)} copy(f32[2,27,6]{1,0,2:T(2,128)} %param.21) | data formatting | bytes 2592 | tf_op args[3]
  1.7 0.2 copy.71
  1.9 0.2 copy.73
  2.1 0.2 copy.75
  2.3 0.2 copy.77
  2.6 0.2 copy.79
  2.8 0.2 copy.81
  3.0 0.4 multiply_add_fusion.1
  3.6 4.2 %multiply_reduce_fusion = f32[2,3,3,128,3,128]{5,3,4,2,1,0:T(8,128)} fusion(f32[2,3,3,3,3,128]{5,4,3,2,1,0:T(4,128)S(1)} %pad_maximum_fusion.2, f32[3,3,128,128]{3,2,1,0:T(8,128)} %constant.164.clone), kind=kLoop, calls=%fused_computation.20 | loop fusion | flops 4423680 | bytes 4211712 | tf_op jit(solution)/shard_map/reduce_sum | solution.py:74
  7.8 3.3 %copy.83 = f32[2,3,3,128,3,128]{3,5,4,2,1,0:T(8,128)S(1)} copy(f32[2,3,3,128,3,128]{5,3,4,2,1,0:T(8,128)} %multiply_reduce_fusion) | data formatting | bytes 7077888 | tf_op jit(solution)/shard_map/reduce_sum | solution.py:74
  11.1 1.0 %pad_bitcast_fusion = f32[2,35,8,128]{3,2,1,0:T(8,128)S(1)} fusion(f32[2,256,128]{2,1,0:T(8,128)} %param.18), kind=kLoop, calls=%fused_computation.37 | loop fusion | bytes 548864 | tf_op jit(solution)/shard_map/reshape | solution.py:58
  12.1 1.8 %fusion.22 = f32[2,32,128,9,8]{2,4,3,1,0:T(8,128)S(1)} fusion(f32[9,8,32,1,1]{2,1,0,4,3:T(8,128)} %constant.174, f32[2,32,8,128]{3,2,1,0:T(8,128)S(1)} %get-tuple-element.185, f32[2,32,8,128]{3,2,1,0:T(8,128)S(1)} %get-tuple-element.186, f32[2,32,8,128]{3,2,1,0:T(8,128)S(1)} %get-tuple-element.187, f32[2,32,8,128]{3,2,1,0:T(8,128)S(1)} %get-tuple-element.184), kind=kOutput, calls=%fused_computation.25 | convolution fusion | flops 114032640 | bytes 3417088 | tf_op jit(solution)/shard_map/kit,nqtx->nqkix/dot_general | solution.py:61
  14.0 2.3 %fusion.19 = f32[2,256,384]{2,1,0:T(8,128)S(1)} fusion(f32[2,9,128,384,1]{2,3,1,4,0:T(8,128)S(1)} %bitcast.101, f32[2,32,128,9,8]{2,4,3,1,0:T(8,128)S(1)} %fusion.22), kind=kOutput, calls=%fused_computation.23 | convolution fusion | flops 1358954496 | bytes 6684672 | tf_op jit(solution)/shard_map/nqkiy,nkyz->nqiz/dot_general | solution.py:76
  16.5 1.1 %select_reduce_fusion = (f32[2]{0:T(128)S(1)}, f32[2]{0:T(128)S(1)}) fusion(pred[2,256,128]{2,1,0:T(32,128)(4,1)S(1)} %get-tuple-element.171, f32[2,256,128]{2,1,0:T(8,128)} %param.19), kind=kLoop, calls=%fused_computation.44 | loop fusion | flops 262140 | bytes 327696 | tf_op jit(solution)/shard_map/reduce_sum | solution.py:134
  18.0 0.8 %fusion.33 = f32[128,3]{0,1:T(4,128)S(1)} fusion(s32[64]{0:T(128)S(1)} %multiply_add_fusion.4, s32[64,1]{0,1:T(1,128)S(1)} %stack_reshape.3, s32[64,1]{0,1:T(1,128)} %bitcast.116, s32[64,1]{0,1:T(1,128)} %bitcast.117), kind=kOutput, calls=%fused_computation.50 | convolution fusion | flops 303680 | bytes 2560 | tf_op jit(solution)/shard_map/dot_general | solution.py:145
  18.9 0.2 fusion.34
  19.4 0.3 scatter.11
  19.7 0.3 scatter.14
  19.9 0.8 %pad_maximum_fusion.1 = f32[8,136,128]{2,1,0:T(8,128)} fusion(f32[8,8,128]{2,1,0:T(8,128)S(1)} %scatter.14, f32[8,128,128]{2,1,0:T(8,128)S(1)} %reshape.332), kind=kLoop, calls=%fused_computation.33 | loop fusion | flops 139264 | bytes 1114112 | tf_op jit(solution)/shard_map/concatenate | solution.py:155
  20.8 7.3 %all-to-all-start = ((f32[8,136,128]{2,1,0:T(8,128)}), f32[8,136,128]{2,1,0:T(8,128)S(1)}, u32[]{:S(2)}, u32[]{:S(2)}) async-start(f32[8,136,128]{2,1,0:T(8,128)} %pad_maximum_fusion.1), calls=%async_computation | async-start | bytes 1114112 | tf_op jit(solution)/shard_map/all_to_all | solution.py:156
  28.1 0.4 fusion.35
  28.7 2.1 %collective-permute-start = (f32[1,128,128]{2,1,0:T(8,128)S(1)}, f32[1,128,128]{2,1,0:T(8,128)S(1)}, u32[]{:S(2)}, u32[]{:S(2)}) collective-permute-start(f32[1,128,128]{2,1,0:T(8,128)S(1)} %get-tuple-element.182), channel_id=1, source_target_pairs={{0,4},{4,0},{8,12},{12,8},{16,20},{20,16},{24,28},{28,24},{1,5},{5... | collective-permute-start | bytes 196616 | tf_op jit(solution)/shard_map/ppermute | solution.py:172
  30.8 1.5 %collective-permute-start.1 = (f32[1,128,128]{2,1,0:T(8,128)S(1)}, f32[1,128,128]{2,1,0:T(8,128)S(1)}, u32[]{:S(2)}, u32[]{:S(2)}) collective-permute-start(f32[1,128,128]{2,1,0:T(8,128)S(1)} %get-tuple-element.181), channel_id=1, source_target_pairs={{0,8},{4,12},{8,0},{12,4},{16,24},{20,28},{24,16},{28,20},{1,9},{5... | collective-permute-start | bytes 196616 | tf_op jit(solution)/shard_map/ppermute | solution.py:172
  32.4 2.8 %collective-permute-start.3 = (f32[1,128,128]{2,1,0:T(8,128)S(1)}, f32[1,128,128]{2,1,0:T(8,128)S(1)}, u32[]{:S(2)}, u32[]{:S(2)}) collective-permute-start(f32[1,128,128]{2,1,0:T(8,128)S(1)} %get-tuple-element.179), channel_id=1, source_target_pairs={{0,16},{4,20},{8,24},{12,28},{16,0},{20,4},{24,8},{28,12},{1,17},{... | collective-permute-start | bytes 196616 | tf_op jit(solution)/shard_map/ppermute | solution.py:172
  35.2 1.5 %collective-permute-start.4 = (f32[1,128,128]{2,1,0:T(8,128)S(1)}, f32[1,128,128]{2,1,0:T(8,128)S(1)}, u32[]{:S(2)}, u32[]{:S(2)}) collective-permute-start(f32[1,128,128]{2,1,0:T(8,128)S(1)} %get-tuple-element.178), channel_id=1, source_target_pairs={{0,20},{4,16},{8,28},{12,24},{16,4},{20,0},{24,12},{28,8},{1,21},{... | collective-permute-start | bytes 196616 | tf_op jit(solution)/shard_map/ppermute | solution.py:172
  36.7 3.3 %collective-permute-start.5 = (f32[1,128,128]{2,1,0:T(8,128)S(1)}, f32[1,128,128]{2,1,0:T(8,128)S(1)}, u32[]{:S(2)}, u32[]{:S(2)}) collective-permute-start(f32[1,128,128]{2,1,0:T(8,128)S(1)} %get-tuple-element.177), channel_id=1, source_target_pairs={{0,24},{4,28},{8,16},{12,20},{16,8},{20,12},{24,0},{28,4},{1,25},{... | collective-permute-start | bytes 196616 | tf_op jit(solution)/shard_map/ppermute | solution.py:172
  40.0 4.6 %collective-permute-start.6 = (f32[1,128,128]{2,1,0:T(8,128)S(1)}, f32[1,128,128]{2,1,0:T(8,128)S(1)}, u32[]{:S(2)}, u32[]{:S(2)}) collective-permute-start(f32[1,128,128]{2,1,0:T(8,128)S(1)} %get-tuple-element.176), channel_id=1, source_target_pairs={{0,28},{4,24},{8,20},{12,16},{16,12},{20,8},{24,4},{28,0},{1,29},{... | collective-permute-start | bytes 196616 | tf_op jit(solution)/shard_map/ppermute | solution.py:172
  44.6 7.1 %collective-permute-done.3 = f32[1,128,128]{2,1,0:T(8,128)S(1)} collective-permute-done((f32[1,128,128]{2,1,0:T(8,128)S(1)}, f32[1,128,128]{2,1,0:T(8,128)S(1)}, u32[]{:S(2)}, u32[]{:S(2)}) %collective-permute-start.3) | collective-permute-done | bytes 65568 | tf_op jit(solution)/shard_map/ppermute | solution.py:172
  51.7 1.9 %collective-permute-done.4 = f32[1,128,128]{2,1,0:T(8,128)S(1)} collective-permute-done((f32[1,128,128]{2,1,0:T(8,128)S(1)}, f32[1,128,128]{2,1,0:T(8,128)S(1)}, u32[]{:S(2)}, u32[]{:S(2)}) %collective-permute-start.4) | collective-permute-done | bytes 65568 | tf_op jit(solution)/shard_map/ppermute | solution.py:172
  54.0 0.2 bitcast_multiply_fusion
  54.3 19.0 %while.16 = (s32[]{:T(128)}, f32[2,128,512]{1,2,0:T(8,128)S(1)}, f32[8,16,2,8,128]{4,3,2,1,0:T(8,128)S(1)}, s32[8,16,2]{1,0,2:T(8,128)S(1)}, s32[]{:T(128)}, /*index=5*/s32[]{:T(128)}) while((s32[]{:T(128)}, f32[2,128,512]{1,2,0:T(8,128)S(1)}, f32[8,16,2,8,128]{4,3,2,1,0:T(8,128)S(1)}, s32[8,16,2]{1,0,2:T(8,128)S(1)}, ...), condition=%wide.region_10.11_spmd.clone.clone, body=%wide.region_9.10_spmd.clone.clone.sunk | while | flops 403982464 | bytes 2246359 | solution.py:118
  54.4 1.5 %fusion.67 = f32[16,2,8,512]{3,2,1,0:T(8,128)S(1)} fusion(s32[16,128]{1,0:T(8,128)S(1)} %iota_add_fusion.4, f32[8,16,2,8,128]{4,3,2,1,0:T(8,128)S(1)} %get-tuple-element.245, s32[]{:T(128)} %get-tuple-element.237), kind=kOutput, calls=%fused_computation.5.clone.1 | convolution fusion | flops 202375168 | bytes 663556 | tf_op jit(solution)/shard_map/while/body/eval_jaxpr/vmwn,vny->vmwy/dot_general | solution.py:108
  56.0 0.7 fusion.68
  56.8 1.5 %fusion.67 = f32[16,2,8,512]{3,2,1,0:T(8,128)S(1)} fusion(s32[16,128]{1,0:T(8,128)S(1)} %iota_add_fusion.4, f32[8,16,2,8,128]{4,3,2,1,0:T(8,128)S(1)} %get-tuple-element.245, s32[]{:T(128)} %get-tuple-element.237), kind=kOutput, calls=%fused_computation.5.clone.1 | convolution fusion | flops 202375168 | bytes 663556 | tf_op jit(solution)/shard_map/while/body/eval_jaxpr/vmwn,vny->vmwy/dot_general | solution.py:108
  58.3 0.7 fusion.68
  59.2 1.5 %fusion.67 = f32[16,2,8,512]{3,2,1,0:T(8,128)S(1)} fusion(s32[16,128]{1,0:T(8,128)S(1)} %iota_add_fusion.4, f32[8,16,2,8,128]{4,3,2,1,0:T(8,128)S(1)} %get-tuple-element.245, s32[]{:T(128)} %get-tuple-element.237), kind=kOutput, calls=%fused_computation.5.clone.1 | convolution fusion | flops 202375168 | bytes 663556 | tf_op jit(solution)/shard_map/while/body/eval_jaxpr/vmwn,vny->vmwy/dot_general | solution.py:108
  60.7 0.7 fusion.68
  61.6 1.5 %fusion.67 = f32[16,2,8,512]{3,2,1,0:T(8,128)S(1)} fusion(s32[16,128]{1,0:T(8,128)S(1)} %iota_add_fusion.4, f32[8,16,2,8,128]{4,3,2,1,0:T(8,128)S(1)} %get-tuple-element.245, s32[]{:T(128)} %get-tuple-element.237), kind=kOutput, calls=%fused_computation.5.clone.1 | convolution fusion | flops 202375168 | bytes 663556 | tf_op jit(solution)/shard_map/while/body/eval_jaxpr/vmwn,vny->vmwy/dot_general | solution.py:108
  63.1 0.7 fusion.68
  63.9 1.5 %fusion.67 = f32[16,2,8,512]{3,2,1,0:T(8,128)S(1)} fusion(s32[16,128]{1,0:T(8,128)S(1)} %iota_add_fusion.4, f32[8,16,2,8,128]{4,3,2,1,0:T(8,128)S(1)} %get-tuple-element.245, s32[]{:T(128)} %get-tuple-element.237), kind=kOutput, calls=%fused_computation.5.clone.1 | convolution fusion | flops 202375168 | bytes 663556 | tf_op jit(solution)/shard_map/while/body/eval_jaxpr/vmwn,vny->vmwy/dot_general | solution.py:108
  65.5 0.7 fusion.68
  66.3 1.5 %fusion.67 = f32[16,2,8,512]{3,2,1,0:T(8,128)S(1)} fusion(s32[16,128]{1,0:T(8,128)S(1)} %iota_add_fusion.4, f32[8,16,2,8,128]{4,3,2,1,0:T(8,128)S(1)} %get-tuple-element.245, s32[]{:T(128)} %get-tuple-element.237), kind=kOutput, calls=%fused_computation.5.clone.1 | convolution fusion | flops 202375168 | bytes 663556 | tf_op jit(solution)/shard_map/while/body/eval_jaxpr/vmwn,vny->vmwy/dot_general | solution.py:108
  67.8 0.7 fusion.68
  68.7 1.5 %fusion.67 = f32[16,2,8,512]{3,2,1,0:T(8,128)S(1)} fusion(s32[16,128]{1,0:T(8,128)S(1)} %iota_add_fusion.4, f32[8,16,2,8,128]{4,3,2,1,0:T(8,128)S(1)} %get-tuple-element.245, s32[]{:T(128)} %get-tuple-element.237), kind=kOutput, calls=%fused_computation.5.clone.1 | convolution fusion | flops 202375168 | bytes 663556 | tf_op jit(solution)/shard_map/while/body/eval_jaxpr/vmwn,vny->vmwy/dot_general | solution.py:108
  70.2 0.7 fusion.68
  71.0 1.5 %fusion.67 = f32[16,2,8,512]{3,2,1,0:T(8,128)S(1)} fusion(s32[16,128]{1,0:T(8,128)S(1)} %iota_add_fusion.4, f32[8,16,2,8,128]{4,3,2,1,0:T(8,128)S(1)} %get-tuple-element.245, s32[]{:T(128)} %get-tuple-element.237), kind=kOutput, calls=%fused_computation.5.clone.1 | convolution fusion | flops 202375168 | bytes 663556 | tf_op jit(solution)/shard_map/while/body/eval_jaxpr/vmwn,vny->vmwy/dot_general | solution.py:108
  72.6 0.7 fusion.68
  73.5 0.8 %slice_divide_fusion = (f32[1,128,512]{2,1,0:T(8,128)}, f32[1,128,512]{2,1,0:T(8,128)}) fusion(f32[2,128,512]{2,1,0:T(8,128)S(1)} %copy.90), kind=kLoop, calls=%fused_computation.38 | loop fusion | flops 131072 | bytes 1048576 | tf_op jit(solution)/shard_map/div | solution.py:190
  (94 shorter events, 3.6 us)
Async XLA Ops:
  14.0 2.3 %copy-start = (s32[2,256,128]{2,1,0:T(8,128)S(1)}, s32[2,256,128]{2,1,0:T(8,128)}, u32[]{:S(2)}) copy-start(s32[2,256,128]{2,1,0:T(8,128)} %param.20) | copy-start | bytes 786436
  14.0 3.7 %copy-start.2 = (s32[64,1]{0,1:T(1,128)S(1)}, s32[64,1]{0,1:T(1,128)}, u32[]{:S(2)}) copy-start(s32[64,1]{0,1:T(1,128)} %param.23) | copy-start | bytes 772
  14.0 3.8 %copy-start.1 = (s32[2,1]{0,1:T(1,128)S(1)}, s32[2,1]{0,1:T(1,128)}, u32[]{:S(2)}) copy-start(s32[2,1]{0,1:T(1,128)} %param.22) | copy-start | bytes 28
  20.8 32.9 %all-to-all-start = ((f32[8,136,128]{2,1,0:T(8,128)}), f32[8,136,128]{2,1,0:T(8,128)S(1)}, u32[]{:S(2)}, u32[]{:S(2)}) async-start(f32[8,136,128]{2,1,0:T(8,128)} %pad_maximum_fusion.1), calls=%async_computation | async-start | bytes 1114112 | tf_op jit(solution)/shard_map/all_to_all | solution.py:156
  28.7 7.9 %collective-permute-start = (f32[1,128,128]{2,1,0:T(8,128)S(1)}, f32[1,128,128]{2,1,0:T(8,128)S(1)}, u32[]{:S(2)}, u32[]{:S(2)}) collective-permute-start(f32[1,128,128]{2,1,0:T(8,128)S(1)} %get-tuple-element.182), channel_id=1, source_target_pairs={{0,4},{4,0},{8,12},{12,8},{16,20},{20,16},{24,28},{28,24},{1,5},{5... | collective-permute-start | bytes 196616 | tf_op jit(solution)/shard_map/ppermute | solution.py:172
  30.8 9.1 %collective-permute-start.1 = (f32[1,128,128]{2,1,0:T(8,128)S(1)}, f32[1,128,128]{2,1,0:T(8,128)S(1)}, u32[]{:S(2)}, u32[]{:S(2)}) collective-permute-start(f32[1,128,128]{2,1,0:T(8,128)S(1)} %get-tuple-element.181), channel_id=1, source_target_pairs={{0,8},{4,12},{8,0},{12,4},{16,24},{20,28},{24,16},{28,20},{1,9},{5... | collective-permute-start | bytes 196616 | tf_op jit(solution)/shard_map/ppermute | solution.py:172
  32.3 12.3 %collective-permute-start.2 = (f32[1,128,128]{2,1,0:T(8,128)S(1)}, f32[1,128,128]{2,1,0:T(8,128)S(1)}, u32[]{:S(2)}, u32[]{:S(2)}) collective-permute-start(f32[1,128,128]{2,1,0:T(8,128)S(1)} %get-tuple-element.180), channel_id=1, source_target_pairs={{0,12},{4,8},{8,4},{12,0},{16,28},{20,24},{24,20},{28,16},{1,13},{... | collective-permute-start | bytes 196616 | tf_op jit(solution)/shard_map/ppermute | solution.py:172
  32.4 19.3 %collective-permute-start.3 = (f32[1,128,128]{2,1,0:T(8,128)S(1)}, f32[1,128,128]{2,1,0:T(8,128)S(1)}, u32[]{:S(2)}, u32[]{:S(2)}) collective-permute-start(f32[1,128,128]{2,1,0:T(8,128)S(1)} %get-tuple-element.179), channel_id=1, source_target_pairs={{0,16},{4,20},{8,24},{12,28},{16,0},{20,4},{24,8},{28,12},{1,17},{... | collective-permute-start | bytes 196616 | tf_op jit(solution)/shard_map/ppermute | solution.py:172
  35.2 18.4 %collective-permute-start.4 = (f32[1,128,128]{2,1,0:T(8,128)S(1)}, f32[1,128,128]{2,1,0:T(8,128)S(1)}, u32[]{:S(2)}, u32[]{:S(2)}) collective-permute-start(f32[1,128,128]{2,1,0:T(8,128)S(1)} %get-tuple-element.178), channel_id=1, source_target_pairs={{0,20},{4,16},{8,28},{12,24},{16,4},{20,0},{24,12},{28,8},{1,21},{... | collective-permute-start | bytes 196616 | tf_op jit(solution)/shard_map/ppermute | solution.py:172
  36.7 16.9 %collective-permute-start.5 = (f32[1,128,128]{2,1,0:T(8,128)S(1)}, f32[1,128,128]{2,1,0:T(8,128)S(1)}, u32[]{:S(2)}, u32[]{:S(2)}) collective-permute-start(f32[1,128,128]{2,1,0:T(8,128)S(1)} %get-tuple-element.177), channel_id=1, source_target_pairs={{0,24},{4,28},{8,16},{12,20},{16,8},{20,12},{24,0},{28,4},{1,25},{... | collective-permute-start | bytes 196616 | tf_op jit(solution)/shard_map/ppermute | solution.py:172
  40.0 13.7 %collective-permute-start.6 = (f32[1,128,128]{2,1,0:T(8,128)S(1)}, f32[1,128,128]{2,1,0:T(8,128)S(1)}, u32[]{:S(2)}, u32[]{:S(2)}) collective-permute-start(f32[1,128,128]{2,1,0:T(8,128)S(1)} %get-tuple-element.176), channel_id=1, source_target_pairs={{0,28},{4,24},{8,20},{12,16},{16,12},{20,8},{24,4},{28,0},{1,29},{... | collective-permute-start | bytes 196616 | tf_op jit(solution)/shard_map/ppermute | solution.py:172
